TPU v7x, 256 devices: a whole 4x4x8 slice. The times are simulated.
256 devices in a mesh: neuron: 32 (over y, z), tm: 2 (over core), trial: 4 (over x).
Axes of the slice: x: 4, y: 4, z: 8, core: 2. Of those that a mesh axis runs over, the one named last changes fastest.
Arguments:
- tensor: bfloat16 [8192, 256, 512], P('neuron', 'tm', 'trial'), may hold values from -6 to 6
- present_blocks: int32 [64, 16], P('neuron'), may hold values 0 or 1
- trial_day: int32 [512], P('trial'), may hold values from 0 to 15
- time_factor: bfloat16 [256, 256], P('tm'), may hold values from 0 to 1
- trial_factor: bfloat16 [512, 256], P('trial'), may hold values from 0 to 1
Outputs:
- neuron_out: bfloat16 [8192, 256], P(('neuron', 'tm', 'trial'))
- time_out: bfloat16 [256, 256], P('tm')
- trial_out: bfloat16 [512, 256], P('trial')
All inputs are finite; a program needn't handle non-finite values. No bound on the sum of `present_blocks` on one device may be relied on, other than what follows from the above.
Results may differ from a plain program's by a relative error of at most 0.0051.
The roundings to bfloat16 on the way count: a program that leaves them out, or rounds other values in their place, can miss the bound.
Values may be sent and summed in bfloat16 or wider, within the bound.
No kernel may reach another device: no remote copies, remote signals or barrier semaphores. Data moves between devices by JAX's collectives and lax.ppermute only.
A program may use at most 128 MiB of HBM per device.

v0:
```python
import jax
import jax.numpy as jnp
from jax import lax
from jax.sharding import PartitionSpec as P

RIDGE = 0.1
EPSILON = 1e-06


def normal_inverse(gram_matrix):
    order_size = gram_matrix.shape[0]
    identity = jnp.eye(order_size, dtype=jnp.float32)
    scaled = gram_matrix / jnp.mean(jnp.diagonal(gram_matrix)) + RIDGE * identity
    lower_factor = jnp.linalg.cholesky(scaled)
    return jax.scipy.linalg.cho_solve((lower_factor, True), identity)


def apply_inverse(partial_sums, inverse):
    return jnp.dot(partial_sums, inverse, precision=lax.Precision.HIGHEST)


def raw_gram(raw_rows):
    return jnp.dot(raw_rows.T, raw_rows, precision=lax.Precision.HIGHEST)


def khatri_rao(left_rows, right_rows):
    return (
        left_rows.astype(jnp.float32)[:, None, :] * right_rows.astype(jnp.float32)[None, :, :]
    ).astype(jnp.bfloat16)


def rescale(raw_rows, gram_sum, total_rows):
    scales = jnp.sqrt(jnp.diagonal(gram_sum) / total_rows + EPSILON)
    factor = (raw_rows / scales[None, :]).astype(jnp.bfloat16)
    normed = gram_sum / (scales[:, None] * scales[None, :])
    return (factor, normed)


def mask_tensor(tensor, present_blocks, trial_day):
    day_count = present_blocks.shape[1]
    onehot = (trial_day[:, None] == jnp.arange(day_count, dtype=jnp.int32)[None, :]).astype(
        jnp.float32
    )
    block_mask = jnp.dot(present_blocks.astype(jnp.float32), onehot.T)
    block_count = present_blocks.shape[0]
    shaped = tensor.reshape(
        block_count, tensor.shape[0] // block_count, tensor.shape[1], tensor.shape[2]
    )
    return shaped * block_mask.astype(jnp.bfloat16)[:, None, None, :]


def factor_gram(rows):
    return jnp.dot(rows.T, rows, preferred_element_type=jnp.float32)


def on_device(tensor, present_blocks, trial_day, time_factor, trial_factor):
    time_all = lax.all_gather(time_factor, "tm", axis=0, tiled=True)
    trial_all = lax.all_gather(trial_factor, "trial", axis=0, tiled=True)
    blocks = mask_tensor(tensor, present_blocks, trial_day)
    block_count, block_rows, time_rows, trial_rows = blocks.shape
    neuron_rows = block_count * block_rows
    flattened = blocks.reshape(neuron_rows, time_rows, trial_rows)
    rank_size = time_factor.shape[1]
    start_time = factor_gram(time_all)
    start_trial = factor_gram(trial_all)
    inverse_neuron = normal_inverse(start_time * start_trial)
    kr_tk = khatri_rao(time_factor, trial_factor)
    neuron_total = neuron_rows * lax.axis_size("neuron")
    block_sums = lax.psum(
        jnp.einsum("itk,tkr->ir", flattened, kr_tk, preferred_element_type=jnp.float32),
        ("tm", "trial"),
    )
    raw_rows = apply_inverse(block_sums, inverse_neuron)
    gram_sum = lax.psum(raw_gram(raw_rows), "neuron")
    neuron_local, gram_neuron = rescale(raw_rows, gram_sum, neuron_total)
    own_rows = neuron_rows // (lax.axis_size("tm") * lax.axis_size("trial"))
    own_index = lax.axis_index("tm") * lax.axis_size("trial") + lax.axis_index("trial")
    neuron_own = lax.dynamic_slice_in_dim(neuron_local, own_index * own_rows, own_rows, axis=0)
    neuron_blocks = neuron_local.reshape(block_count, block_rows, rank_size)
    time_total = time_rows * lax.axis_size("tm")
    inverse_time = normal_inverse(gram_neuron * start_trial)

    def time_add_block(running, inputs):
        tensor_piece, rows_a = inputs
        kr_ik = khatri_rao(rows_a, trial_factor)
        return (
            running
            + jnp.einsum("itk,ikr->tr", tensor_piece, kr_ik, preferred_element_type=jnp.float32),
            None,
        )

    running, unused = lax.scan(
        time_add_block, jnp.zeros((time_rows, rank_size), jnp.float32), (blocks, neuron_blocks)
    )
    half_sums = lax.psum(running, ("neuron", "trial"))
    raw_rows = apply_inverse(half_sums, inverse_time)
    gram_sum = lax.psum(raw_gram(raw_rows), "tm")
    time_local, gram_time = rescale(raw_rows, gram_sum, time_total)
    trial_total = trial_rows * lax.axis_size("trial")
    inverse_trial = normal_inverse(gram_neuron * gram_time)

    def trial_add_block(running, inputs):
        tensor_piece, rows_a = inputs
        kr_it = khatri_rao(rows_a, time_local)
        return (
            running
            + jnp.einsum("itk,itr->kr", tensor_piece, kr_it, preferred_element_type=jnp.float32),
            None,
        )

    running, unused = lax.scan(
        trial_add_block, jnp.zeros((trial_rows, rank_size), jnp.float32), (blocks, neuron_blocks)
    )
    quarter_sums = lax.psum(running, ("neuron", "tm"))
    raw_rows = apply_inverse(quarter_sums, inverse_trial)
    squares = lax.psum(jnp.sum(raw_rows * raw_rows, axis=0), "trial")
    scales = jnp.sqrt(squares / trial_total + EPSILON)
    trial_local = (raw_rows / scales[None, :]).astype(jnp.bfloat16)
    return (neuron_own, time_local, trial_local)


def solution(mesh):
    return jax.shard_map(
        on_device,
        mesh=mesh,
        in_specs=(
            P("neuron", "tm", "trial"),
            P("neuron", None),
            P("trial"),
            P("tm", None),
            P("trial", None),
        ),
        out_specs=(P(("neuron", "tm", "trial"), None), P("tm", None), P("trial", None)),
        check_vma=False,
    )
```

profile of v0, /device:TPU:1, one launch (start us, length us, event | category | flops | bytes accessed | tf_op | source)
XLA Modules:
  0.0 862.3 jit_solution(6178857749009200221)
XLA Ops:
  9.9 7.2 broadcast_multiply_fusion.1
  17.1 9.9 %fusion.28 = f32[256,256]{1,0:T(8,128)} fusion(f32[128,256]{1,0:T(8,128)S(1)} %convert_element_type.81, f32[128,256]{1,0:T(8,128)S(1)} %convert_element_type.80, bf16[256,128,128]{2,1,0:T(8,128)(2,1)} %broadcast_multiply_fusion.1), kind=kOutput, calls=%fused_computation.39 | convolution fusion | flops 2155872256 | bytes 8912896 | tf_op jit(solution)/shard_map/itk,tkr->ir/dot_general | solution.py:70
  27.1 11.0 %all_gather.7 = bf16[512,256]{1,0:T(8,128)(2,1)S(1)} all-gather(bf16[128,256]{1,0:T(8,128)(2,1)S(1)} %copy-done.1), channel_id=1, replica_groups=mesh['neuron'=32,'tm'=2,'trial'=4] {'trial'}, dimensions={0}, use_global_device_ids=true | all-gather | bytes 327680 | tf_op jit(solution)/shard_map/all_gather | solution.py:58
  38.1 6.3 all_gather.6
  44.4 11.9 %copy.27 = bf16[256,128,128]{1,2,0:T(8,128)(2,1)} copy(bf16[256,128,128]{2,1,0:T(8,128)(2,1)} %param.12) | data formatting | bytes 16777216 | tf_op args[0]
  60.7 11.7 %cholesky.172 = f32[128,128]{1,0:T(8,128)S(1)} custom-call(f32[128,128]{1,0:T(8,128)S(1)} %cholesky.270), custom_call_target="Cholesky" | custom-call | tf_op jit(solution)/shard_map/jit(cholesky)/cholesky | solution.py:14
  72.5 9.8 %custom-call.29 = f32[1,128,128]{1,2,0:T(8,128)S(1)} custom-call(f32[1,128,128]{2,1,0:T(8,128)S(1)} %get-tuple-element.207), custom_call_target="InvertDiagBlocksLowerTriangular" | custom-call | tf_op jit(solution)/shard_map/jit(cholesky)/cholesky | solution.py:14
  82.8 11.7 %cholesky.189 = f32[128,128]{1,0:T(8,128)S(1)} custom-call(f32[128,128]{1,0:T(8,128)S(1)} %convolution_subtract_fusion.8), custom_call_target="Cholesky" | custom-call | tf_op jit(solution)/shard_map/jit(cholesky)/cholesky | solution.py:14
  96.6 4.0 while.30
  100.6 19.9 %custom-call.30 = f32[2,128,128]{1,2,0:T(8,128)S(1)} custom-call(f32[2,128,128]{2,1,0:T(8,128)S(1)} %get-tuple-element.117), custom_call_target="InvertDiagBlocksLowerTriangular" | custom-call | tf_op jit(solution)/shard_map/jit(_cho_solve)/triangular_solve | solution.py:15
  125.1 7.2 broadcast_multiply_fusion
  132.5 134.6 %all-reduce.9.cloned.1.call-done = f32[256,256]{0,1:T(8,128)} async-done(((f32[256,256]{0,1:T(8,128)}), f32[256,256]{0,1:T(8,128)}) %all-reduce.9.cloned.1.call-update) | async-done | bytes 262160 | tf_op jit(solution)/shard_map/psum | solution.py:74
  274.7 11.7 %cholesky.206 = f32[128,128]{1,0:T(8,128)S(1)} custom-call(f32[128,128]{1,0:T(8,128)S(1)} %cholesky.273), custom_call_target="Cholesky" | custom-call | tf_op jit(solution)/shard_map/jit(cholesky)/cholesky | solution.py:14
  286.5 9.8 %custom-call.31 = f32[1,128,128]{1,2,0:T(8,128)S(1)} custom-call(f32[1,128,128]{2,1,0:T(8,128)S(1)} %get-tuple-element.203), custom_call_target="InvertDiagBlocksLowerTriangular" | custom-call | tf_op jit(solution)/shard_map/jit(cholesky)/cholesky | solution.py:14
  296.8 11.7 %cholesky.223 = f32[128,128]{1,0:T(8,128)S(1)} custom-call(f32[128,128]{1,0:T(8,128)S(1)} %convolution_subtract_fusion.7), custom_call_target="Cholesky" | custom-call | tf_op jit(solution)/shard_map/jit(cholesky)/cholesky | solution.py:14
  311.0 3.8 while.31
  314.9 20.1 %custom-call.32 = f32[2,128,128]{1,2,0:T(8,128)S(1)} custom-call(f32[2,128,128]{2,1,0:T(8,128)S(1)} %get-tuple-element.118), custom_call_target="InvertDiagBlocksLowerTriangular" | custom-call | tf_op jit(solution)/shard_map/jit(_cho_solve)/triangular_solve | solution.py:15
  336.7 7.4 while.28
  336.8 3.6 fusion.130
  340.5 3.6 fusion.130
  345.1 211.7 %all-reduce.11.cloned.1.call-done = f32[128,256]{1,0:T(8,128)} async-done(((f32[128,256]{1,0:T(8,128)}), f32[128,256]{1,0:T(8,128)}) %all-reduce.11.cloned.1.call-update) | async-done | bytes 131088 | tf_op jit(solution)/shard_map/psum | solution.py:95
  559.9 31.0 %all-reduce.13.cloned.1.call-done = f32[256,256]{0,1:T(8,128)} async-done(((f32[256,256]{0,1:T(8,128)}), f32[256,256]{0,1:T(8,128)}) %all-reduce.13.cloned.1.call-update) | async-done | bytes 262160 | tf_op jit(solution)/shard_map/psum | solution.py:97
  598.6 11.7 %cholesky.240 = f32[128,128]{1,0:T(8,128)S(1)} custom-call(f32[128,128]{1,0:T(8,128)S(1)} %cholesky.276), custom_call_target="Cholesky" | custom-call | tf_op jit(solution)/shard_map/jit(cholesky)/cholesky | solution.py:14
  610.4 9.8 %custom-call.33 = f32[1,128,128]{1,2,0:T(8,128)S(1)} custom-call(f32[1,128,128]{2,1,0:T(8,128)S(1)} %get-tuple-element.199), custom_call_target="InvertDiagBlocksLowerTriangular" | custom-call | tf_op jit(solution)/shard_map/jit(cholesky)/cholesky | solution.py:14
  620.7 11.7 %cholesky.257 = f32[128,128]{1,0:T(8,128)S(1)} custom-call(f32[128,128]{1,0:T(8,128)S(1)} %convolution_subtract_fusion.6), custom_call_target="Cholesky" | custom-call | tf_op jit(solution)/shard_map/jit(cholesky)/cholesky | solution.py:14
  635.0 3.7 while.32
  638.7 19.9 %custom-call.34 = f32[2,128,128]{1,2,0:T(8,128)S(1)} custom-call(f32[2,128,128]{2,1,0:T(8,128)S(1)} %get-tuple-element.119), custom_call_target="InvertDiagBlocksLowerTriangular" | custom-call | tf_op jit(solution)/shard_map/jit(_cho_solve)/triangular_solve | solution.py:15
  660.3 7.2 while.29
  660.3 3.5 fusion.132
  663.9 3.5 fusion.132
  668.4 176.9 %all-reduce.15.cloned.1.call-done = f32[128,256]{1,0:T(8,128)} async-done(((f32[128,256]{1,0:T(8,128)}), f32[128,256]{1,0:T(8,128)}) %all-reduce.15.cloned.1.call-update) | async-done | bytes 131088 | tf_op jit(solution)/shard_map/psum | solution.py:114
  846.5 8.4 psum.47
  (141 shorter events, 51.8 us)
Async XLA Ops:
  7.2 115.3 %all-reduce.7.cloned.1.call-start = ((), (), s32[]{:S(2)}) async-start(), calls=%async_computation | async-start | bytes 524288 | tf_op jit(solution)/shard_map/psum | solution.py:69
  17.0 10.0 %copy-start.1 = (bf16[128,256]{1,0:T(8,128)(2,1)S(1)}, bf16[128,256]{1,0:T(8,128)(2,1)}, u32[]{:S(2)}) copy-start(bf16[128,256]{1,0:T(8,128)(2,1)} %param.16) | copy-start | bytes 196612
  17.1 21.0 %copy-start.3 = (bf16[128,256]{1,0:T(8,128)(2,1)S(1)}, bf16[128,256]{1,0:T(8,128)(2,1)}, u32[]{:S(2)}) copy-start(bf16[128,256]{1,0:T(8,128)(2,1)} %param.15) | copy-start | bytes 196612
  27.0 240.1 %all-reduce.9.cloned.1.call-start = ((), (), s32[]{:S(2)}) async-start(), calls=%async_computation.1 | async-start | bytes 524288 | tf_op jit(solution)/shard_map/psum | solution.py:74
  125.1 431.6 %all-reduce.11.cloned.1.call-start = ((), (), s32[]{:S(2)}) async-start(), calls=%async_computation.2 | async-start | bytes 262144 | tf_op jit(solution)/shard_map/psum | solution.py:95
  336.7 256.9 %copy-start = (f32[256,256]{0,1:T(8,128)S(1)}, f32[256,256]{0,1:T(8,128)}, u32[]{:S(2)}) copy-start(f32[256,256]{0,1:T(8,128)} %all-reduce.9.cloned.1.call-done) | copy-start | bytes 786436
  344.1 0.6 copy-start.5
  344.8 246.2 %all-reduce.13.cloned.1.call-start = ((), (), s32[]{:S(2)}) async-start(), calls=%async_computation.3 | async-start | bytes 524288 | tf_op jit(solution)/shard_map/psum | solution.py:97
  559.1 286.2 %all-reduce.15.cloned.1.call-start = ((), (), s32[]{:S(2)}) async-start(), calls=%async_computation.4 | async-start | bytes 262144 | tf_op jit(solution)/shard_map/psum | solution.py:114
  667.5 0.7 copy-start.4
  667.5 188.1 %copy-start.2 = (bf16[128,256]{1,0:T(8,128)(2,1)}, bf16[128,256]{1,0:T(8,128)(2,1)S(1)}, u32[]{:S(2)}) copy-start(bf16[128,256]{1,0:T(8,128)(2,1)S(1)} %get-tuple-element.465) | copy-start | bytes 196612
Sparse Core Ops, SparseCore 0:
  27.1 67.1 all-reduce.6
  125.2 141.8 all-reduce.8
  344.9 211.8 all-reduce.10
  559.2 31.7 all-reduce.12
  668.3 176.9 all-reduce.14
where the time goes:
time: 867 us; the launch traced here: 862 us
  waiting for transfers between devices  554 us (64%)
  other arithmetic  184 us (21%)
  matrix products  38.7 us (4%)
  local copies, waits for them, and re-layouts  38.7 us (4%)
  blocking collectives  25.7 us (3%)
  between operations  20.2 us (2%)
    psum x1, waiting for transfers between devices, on_device(): half_sums = lax.psum(running, ('neuron', 'trial'))  212 us
    psum x1, waiting for transfers between devices, on_device(): quarter_sums = lax.psum(running, ('neuron', 'tm'))  177 us
    psum x1, waiting for transfers between devices, on_device(): gram_sum = lax.psum(raw_gram(raw_rows), 'neuron')  135 us
    another operation x20, other arithmetic, normal_inverse(): lower_factor = jnp.linalg.cholesky(scaled)  103 us
    another operation x7, other arithmetic, normal_inverse(): return jax.scipy.linalg.cho_solve((lower_factor, True), identity)  59.9 us
    psum x1, waiting for transfers between devices, on_device(): gram_sum = lax.psum(raw_gram(raw_rows), 'tm')  31 us
  transfers between devices with their start and end apart: 5, of which 4 were waited for; matrix products, arithmetic and copies ran while one was open for 10% of the time, Pallas kernels for 0%

commit v1 on v0

--- a/solution.py
+++ b/solution.py
@@ -92,7 +92,8 @@
     running, unused = lax.scan(
         time_add_block, jnp.zeros((time_rows, rank_size), jnp.float32), (blocks, neuron_blocks)
     )
-    half_sums = lax.psum(running, ("neuron", "trial"))
+    local_out = lax.all_gather(running, axis_name=("neuron", "trial"))
+    half_sums = jnp.sum(local_out, axis=0)
     raw_rows = apply_inverse(half_sums, inverse_time)
     gram_sum = lax.psum(raw_gram(raw_rows), "tm")
     time_local, gram_time = rescale(raw_rows, gram_sum, time_total)

time: 867 us -> 677 us (0.78)
  waiting for transfers between devices: 554 us -> 358 us
    psum x1 -> x0, waiting for transfers between devices: 212 us -> none  [on_device(): half_sums = lax.psum(running, ('neuron', 'trial'))]
    all_gather x0 -> x1, waiting for transfers between devices: none -> 85.4 us  [on_device(): local_out = lax.all_gather(running, axis_name=('neuron', 'trial'))]
    psum x1, waiting for transfers between devices: 177 us -> 111 us  [on_device(): quarter_sums = lax.psum(running, ('neuron', 'tm'))]
  transfers between devices with their start and end apart: 5 -> 5, of which waited for: 4 -> 4; matrix products, arithmetic and copies ran while one was open for 10% -> 32% of each run, Pallas kernels for 0% -> 0%
where the time goes in v1:
time: 677 us; the launch traced here: 672 us
  waiting for transfers between devices  358 us (53%)
  other arithmetic  190 us (28%)
  local copies, waits for them, and re-layouts  39.5 us (6%)
  matrix products  37.8 us (6%)
  blocking collectives  25.7 us (4%)
  between operations  20.4 us (3%)
    psum x1, waiting for transfers between devices, on_device(): gram_sum = lax.psum(raw_gram(raw_rows), 'neuron')  135 us
    psum x1, waiting for transfers between devices, on_device(): quarter_sums = lax.psum(running, ('neuron', 'tm'))  111 us
    another operation x20, other arithmetic, normal_inverse(): lower_factor = jnp.linalg.cholesky(scaled)  103 us
    all_gather x1, waiting for transfers between devices, on_device(): local_out = lax.all_gather(running, axis_name=('neuron', 'trial'))  85.4 us
    another operation x7, other arithmetic, normal_inverse(): return jax.scipy.linalg.cho_solve((lower_factor, True), identity)  59.8 us
    psum x1, waiting for transfers between devices, on_device(): gram_sum = lax.psum(raw_gram(raw_rows), 'tm')  26.9 us
    mul x2, other arithmetic, mask_tensor(): return shaped * block_mask.astype(jnp.bfloat16)[:, None, None, :]  14.4 us
    unnamed x17, local copies, waits for them, and re-layouts  14 us
  transfers between devices with their start and end apart: 5, of which 4 were waited for; matrix products, arithmetic and copies ran while one was open for 32% of the time, Pallas kernels for 0%

profile of v1, /device:TPU:1, one launch (start us, length us, event | category | flops | bytes accessed | tf_op | source)
XLA Modules:
  0.0 671.9 jit_solution(14465821176167481692)
XLA Ops:
  9.9 7.2 %broadcast_multiply_fusion.1 = bf16[256,128,128]{2,1,0:T(8,128)(2,1)} fusion(bf16[256,128,128]{2,1,0:T(8,128)(2,1)} %param.12, bf16[256,128]{1,0:T(8,128)(2,1)S(1)} %bitcast.177), kind=kLoop, calls=%fused_computation.37 | loop fusion | flops 4194304 | bytes 16842752 | tf_op jit(solution)/shard_map/mul | solution.py:49
  17.1 10.0 %fusion.28 = f32[256,256]{1,0:T(8,128)} fusion(f32[128,256]{1,0:T(8,128)S(1)} %convert_element_type.81, f32[128,256]{1,0:T(8,128)S(1)} %convert_element_type.80, bf16[256,128,128]{2,1,0:T(8,128)(2,1)} %broadcast_multiply_fusion.1), kind=kOutput, calls=%fused_computation.39 | convolution fusion | flops 2155872256 | bytes 8912896 | tf_op jit(solution)/shard_map/itk,tkr->ir/dot_general | solution.py:70
  27.1 11.0 %all_gather.13 = bf16[512,256]{1,0:T(8,128)(2,1)S(1)} all-gather(bf16[128,256]{1,0:T(8,128)(2,1)S(1)} %copy-done.2), channel_id=1, replica_groups=mesh['neuron'=32,'tm'=2,'trial'=4] {'trial'}, dimensions={0}, use_global_device_ids=true | all-gather | bytes 327680 | tf_op jit(solution)/shard_map/all_gather | solution.py:58
  38.1 6.3 all_gather.12
  44.5 11.9 %copy.27 = bf16[256,128,128]{1,2,0:T(8,128)(2,1)} copy(bf16[256,128,128]{2,1,0:T(8,128)(2,1)} %param.12) | data formatting | bytes 16777216 | tf_op args[0]
  60.8 11.7 %cholesky.172 = f32[128,128]{1,0:T(8,128)S(1)} custom-call(f32[128,128]{1,0:T(8,128)S(1)} %cholesky.270), custom_call_target="Cholesky" | custom-call | tf_op jit(solution)/shard_map/jit(cholesky)/cholesky | solution.py:14
  72.6 9.8 %custom-call.29 = f32[1,128,128]{1,2,0:T(8,128)S(1)} custom-call(f32[1,128,128]{2,1,0:T(8,128)S(1)} %get-tuple-element.207), custom_call_target="InvertDiagBlocksLowerTriangular" | custom-call | tf_op jit(solution)/shard_map/jit(cholesky)/cholesky | solution.py:14
  82.9 11.7 %cholesky.189 = f32[128,128]{1,0:T(8,128)S(1)} custom-call(f32[128,128]{1,0:T(8,128)S(1)} %convolution_subtract_fusion.8), custom_call_target="Cholesky" | custom-call | tf_op jit(solution)/shard_map/jit(cholesky)/cholesky | solution.py:14
  96.7 4.0 while.30
  100.7 19.9 %custom-call.30 = f32[2,128,128]{1,2,0:T(8,128)S(1)} custom-call(f32[2,128,128]{2,1,0:T(8,128)S(1)} %get-tuple-element.117), custom_call_target="InvertDiagBlocksLowerTriangular" | custom-call | tf_op jit(solution)/shard_map/jit(_cho_solve)/triangular_solve | solution.py:15
  125.2 7.2 %broadcast_multiply_fusion = bf16[2,128,128,128]{2,3,1,0:T(8,128)(2,1)} fusion(bf16[2,128,128,128]{2,3,1,0:T(8,128)(2,1)} %bitcast.174, bf16[2,128]{1,0:T(2,128)(2,1)S(1)} %fusion.31), kind=kLoop, calls=%fused_computation.36 | loop fusion | flops 4194304 | bytes 16777728 | tf_op jit(solution)/shard_map/mul | solution.py:49
  132.6 134.6 %all-reduce.8.cloned.1.call-done = f32[256,256]{0,1:T(8,128)} async-done(((f32[256,256]{0,1:T(8,128)}), f32[256,256]{0,1:T(8,128)}) %all-reduce.8.cloned.1.call-update) | async-done | bytes 262160 | tf_op jit(solution)/shard_map/psum | solution.py:74
  271.0 7.4 %while.28 = (s32[]{:T(128)}, f32[128,256]{1,0:T(8,128)S(1)}, bf16[2,128,128,128]{2,3,1,0:T(8,128)(2,1)}, bf16[2,128,256]{2,1,0:T(8,128)(2,1)S(1)}, bf16[128,256]{1,0:T(8,128)(2,1)S(1)}, /*index=5*/s32[]{:T(128)}, s32[]{:T(128)}) while((s32[]{:T(128)}, f32[128,256]{1,0:T(8,128)S(1)}, bf16[2,128,128,128]{2,3,1,0:T(8,128)(2,1)}, ...), condition=%wide.region_8.11_spmd.clone, body=%wide.region_7.10_spmd.clone.sunk | while | flops 1082261504 | bytes 5111911 | solution.py:92
  271.1 3.6 fusion.130
  274.7 3.6 fusion.130
  283.4 11.7 %cholesky.206 = f32[128,128]{1,0:T(8,128)S(1)} custom-call(f32[128,128]{1,0:T(8,128)S(1)} %cholesky.273), custom_call_target="Cholesky" | custom-call | tf_op jit(solution)/shard_map/jit(cholesky)/cholesky | solution.py:14
  295.2 9.8 %custom-call.31 = f32[1,128,128]{1,2,0:T(8,128)S(1)} custom-call(f32[1,128,128]{2,1,0:T(8,128)S(1)} %get-tuple-element.203), custom_call_target="InvertDiagBlocksLowerTriangular" | custom-call | tf_op jit(solution)/shard_map/jit(cholesky)/cholesky | solution.py:14
  305.5 11.7 %cholesky.223 = f32[128,128]{1,0:T(8,128)S(1)} custom-call(f32[128,128]{1,0:T(8,128)S(1)} %convolution_subtract_fusion.7), custom_call_target="Cholesky" | custom-call | tf_op jit(solution)/shard_map/jit(cholesky)/cholesky | solution.py:14
  319.7 3.8 while.31
  323.6 19.8 %custom-call.32 = f32[2,128,128]{1,2,0:T(8,128)S(1)} custom-call(f32[2,128,128]{2,1,0:T(8,128)S(1)} %get-tuple-element.118), custom_call_target="InvertDiagBlocksLowerTriangular" | custom-call | tf_op jit(solution)/shard_map/jit(_cho_solve)/triangular_solve | solution.py:15
  345.3 85.4 %all-gather.3.cloned.1.call-done = f32[16384,256]{1,0:T(8,128)} async-done(((f32[128,256]{1,0:T(8,128)}), f32[16384,256]{1,0:T(8,128)}) %all-gather.3.cloned.1.call-update) | async-done | bytes 16777232 | tf_op jit(solution)/shard_map/all_gather | solution.py:95
  430.7 6.8 %reduce_sum.46 = f32[128,256]{1,0:T(8,128)S(1)} reduce(f32[128,128,256]{2,1,0:T(8,128)} %bitcast.175, f32[]{:T(128)} %constant.118.clone.1), dimensions={0}, to_apply=%region_9.12 | reduce | flops 4161536 | bytes 16908292 | tf_op jit(solution)/shard_map/reduce_sum | solution.py:96
  439.8 26.9 %all-reduce.10.cloned.1.call-done = f32[256,256]{0,1:T(8,128)} async-done(((f32[256,256]{0,1:T(8,128)}), f32[256,256]{0,1:T(8,128)}) %all-reduce.10.cloned.1.call-update) | async-done | bytes 262160 | tf_op jit(solution)/shard_map/psum | solution.py:98
  469.3 7.2 %while.29 = (s32[]{:T(128)}, f32[128,256]{1,0:T(8,128)S(1)}, bf16[2,128,128,128]{2,3,1,0:T(8,128)(2,1)}, bf16[2,128,256]{2,1,0:T(8,128)(2,1)S(1)}, bf16[128,256]{1,0:T(8,128)(2,1)S(1)}, /*index=5*/s32[]{:T(128)}, s32[]{:T(128)}) while((s32[]{:T(128)}, f32[128,256]{1,0:T(8,128)S(1)}, bf16[2,128,128,128]{2,3,1,0:T(8,128)(2,1)}, ...), condition=%wide.region_13.16_spmd.clone, body=%wide.region_12.15_spmd.clone.sunk | while | flops 1082261504 | bytes 5111911 | solution.py:112
  469.3 3.6 fusion.132
  481.6 11.7 %cholesky.240 = f32[128,128]{1,0:T(8,128)S(1)} custom-call(f32[128,128]{1,0:T(8,128)S(1)} %cholesky.276), custom_call_target="Cholesky" | custom-call | tf_op jit(solution)/shard_map/jit(cholesky)/cholesky | solution.py:14
  493.4 9.8 %custom-call.33 = f32[1,128,128]{1,2,0:T(8,128)S(1)} custom-call(f32[1,128,128]{2,1,0:T(8,128)S(1)} %get-tuple-element.199), custom_call_target="InvertDiagBlocksLowerTriangular" | custom-call | tf_op jit(solution)/shard_map/jit(cholesky)/cholesky | solution.py:14
  503.7 11.7 %cholesky.257 = f32[128,128]{1,0:T(8,128)S(1)} custom-call(f32[128,128]{1,0:T(8,128)S(1)} %convolution_subtract_fusion.6), custom_call_target="Cholesky" | custom-call | tf_op jit(solution)/shard_map/jit(cholesky)/cholesky | solution.py:14
  518.1 4.1 while.32
  522.2 19.9 %custom-call.34 = f32[2,128,128]{1,2,0:T(8,128)S(1)} custom-call(f32[2,128,128]{2,1,0:T(8,128)S(1)} %get-tuple-element.119), custom_call_target="InvertDiagBlocksLowerTriangular" | custom-call | tf_op jit(solution)/shard_map/jit(_cho_solve)/triangular_solve | solution.py:15
  544.0 110.9 %all-reduce.12.cloned.1.call-done = f32[128,256]{1,0:T(8,128)} async-done(((f32[128,256]{1,0:T(8,128)}), f32[128,256]{1,0:T(8,128)}) %all-reduce.12.cloned.1.call-update) | async-done | bytes 131088 | tf_op jit(solution)/shard_map/psum | solution.py:115
  656.1 8.4 %psum.39 = f32[256]{0:T(256)S(1)} all-reduce(f32[256]{0:T(256)S(1)} %get-tuple-element.216), channel_id=1, replica_groups=mesh['neuron'=32,'tm'=2,'trial'=4] {'trial'}, use_global_device_ids=true, to_apply=%region_17.20 | all-reduce | flops 256 | bytes 2048 | tf_op jit(solution)/shard_map/psum | solution.py:117
  (144 shorter events, 54.4 us)
Async XLA Ops:
  7.2 115.3 %all-reduce.6.cloned.1.call-start = ((), (), s32[]{:S(2)}) async-start(), calls=%async_computation | async-start | bytes 524288 | tf_op jit(solution)/shard_map/psum | solution.py:69
  17.0 10.0 %copy-start.2 = (bf16[128,256]{1,0:T(8,128)(2,1)S(1)}, bf16[128,256]{1,0:T(8,128)(2,1)}, u32[]{:S(2)}) copy-start(bf16[128,256]{1,0:T(8,128)(2,1)} %param.16) | copy-start | bytes 196612
  17.1 21.1 %copy-start.4 = (bf16[128,256]{1,0:T(8,128)(2,1)S(1)}, bf16[128,256]{1,0:T(8,128)(2,1)}, u32[]{:S(2)}) copy-start(bf16[128,256]{1,0:T(8,128)(2,1)} %param.15) | copy-start | bytes 196612
  27.0 240.1 %all-reduce.8.cloned.1.call-start = ((), (), s32[]{:S(2)}) async-start(), calls=%async_computation.1 | async-start | bytes 524288 | tf_op jit(solution)/shard_map/psum | solution.py:74
  125.2 305.5 %all-gather.3.cloned.1.call-start = ((), (), s32[]{:S(2)}) async-start(), calls=%async_computation.4 | async-start | bytes 16908288 | tf_op jit(solution)/shard_map/all_gather | solution.py:95
  278.4 0.6 copy-start.6
  279.0 187.6 %all-reduce.10.cloned.1.call-start = ((), (), s32[]{:S(2)}) async-start(), calls=%async_computation.2 | async-start | bytes 524288 | tf_op jit(solution)/shard_map/psum | solution.py:98
  438.9 216.0 %all-reduce.12.cloned.1.call-start = ((), (), s32[]{:S(2)}) async-start(), calls=%async_computation.3 | async-start | bytes 262144 | tf_op jit(solution)/shard_map/psum | solution.py:115
  469.3 7.9 %copy-start = (f32[256,256]{0,1:T(8,128)S(1)}, f32[256,256]{0,1:T(8,128)}, u32[]{:S(2)}) copy-start(f32[256,256]{0,1:T(8,128)} %all-reduce.8.cloned.1.call-done) | copy-start | bytes 786436
  469.3 7.9 %copy-start.1 = (f32[256,256]{0,1:T(8,128)S(1)}, f32[256,256]{0,1:T(8,128)}, u32[]{:S(2)}) copy-start(f32[256,256]{0,1:T(8,128)} %all-reduce.10.cloned.1.call-done) | copy-start | bytes 786436
  476.5 0.7 copy-start.5
  476.5 188.6 %copy-start.3 = (bf16[128,256]{1,0:T(8,128)(2,1)}, bf16[128,256]{1,0:T(8,128)(2,1)S(1)}, u32[]{:S(2)}) copy-start(bf16[128,256]{1,0:T(8,128)(2,1)S(1)} %get-tuple-element.466) | copy-start | bytes 196612
Sparse Core Ops, SparseCore 0:
  27.2 67.2 all-reduce.5
  125.3 141.8 all-reduce.7
  279.2 151.4 all-gather.2
  439.0 27.5 all-reduce.9
  477.3 177.4 all-reduce.11
